TPU v7x, 128 devices: a whole 4x4x4 slice. The times are simulated.
128 devices in a mesh: req: 16 (over y, z), mp: 8 (over x, core).
Axes of the slice: x: 4, y: 4, z: 4, core: 2. Of those that a mesh axis runs over, the one named last changes fastest.
Arguments:
- hidden_in: bfloat16 [16384, 2048], P('req', 'mp'), may hold values from -6 to 6
- w_qkv: bfloat16 [3, 2048, 2048], P(None, 'req', 'mp'), may hold values from -0.125 to 0.125
- w_out: bfloat16 [2048, 2048], P('mp', 'req'), may hold values from -0.125 to 0.125
- attn_gain: bfloat16 [2048], replicated, may hold values from 0.099609375 to 1.8984375
- mlp_gain: bfloat16 [2048], replicated, may hold values from 0.099609375 to 1.8984375
- w_gate: bfloat16 [2048, 8192], P('req', 'mp'), may hold values from -0.125 to 0.125
- w_up: bfloat16 [2048, 8192], P('req', 'mp'), may hold values from -0.125 to 0.125
- w_down: bfloat16 [8192, 2048], P('mp', 'req'), may hold values from -0.0625 to 0.0625
- k_cache: bfloat16 [16, 4096, 2048], P('req', None, 'mp'), may hold values from -363 to 363
- v_cache: bfloat16 [16, 4096, 2048], P('req', None, 'mp'), may hold values from -6 to 6
- cache_len: int32 [16], P('req'), may hold values from 256 to 4096, as said below
Outputs:
- hidden_out: bfloat16 [16384, 2048], P('req', 'mp')
- new_keys: bfloat16 [16384, 2048], P('req', 'mp')
- new_values: bfloat16 [16384, 2048], P('req', 'mp')
Inputs may be any that keep to these rules, and one draw needn't show every extreme that they name: Each request uses its first cache_len slots; later slots hold unused data. Some request's cache is full in every draw.
All inputs are finite; a program needn't handle non-finite values.
Results may differ from a plain program's by a relative error of at most 0.02.
Values may be sent and summed in bfloat16 or wider, within the bound.
No kernel may reach another device: no remote copies, remote signals or barrier semaphores. Data moves between devices by JAX's collectives and lax.ppermute only.
A program may use at most 128 MiB of HBM per device.

v0:
```python
import jax
import jax.numpy as jnp
from jax import lax
from jax.sharding import PartitionSpec as P

HD = 64
THETA = 130000.0
EPSILON = 1e-05
NEG_FILL = -1e30


def rms_scale(rows, gain):
    values = rows.astype(jnp.float32)
    meansq = jnp.mean(values * values, axis=-1, keepdims=True)
    return (values * lax.rsqrt(meansq + EPSILON) * gain.astype(jnp.float32)).astype(jnp.bfloat16)


def rotate(tensor, positions):
    half = tensor.shape[-1] // 2
    freq = THETA ** (-(jnp.arange(half, dtype=jnp.float32) * 2.0 / tensor.shape[-1]))
    angle = positions[:, None, None] * freq[None, None, :]
    cosine = jnp.cos(angle)
    sine = jnp.sin(angle)
    first = tensor[..., :half]
    second = tensor[..., half:]
    return jnp.concatenate(
        [first * cosine - second * sine, second * cosine + first * sine], axis=-1
    )


def gather_packed(blocks, axes, axis_name):
    count = lax.axis_size(axis_name)
    lane = 128
    joined = jnp.concatenate([block.reshape(-1, lane) for block in blocks], axis=0)
    gathered = lax.all_gather(joined, axis_name, axis=0, tiled=False)
    outs = []
    offset = 0
    for block, axis in zip(blocks, axes):
        rows = block.size // lane
        piece = gathered[:, offset : offset + rows].reshape((count,) + block.shape)
        piece = jnp.moveaxis(piece, 0, axis)
        shape = list(block.shape)
        shape[axis] *= count
        outs.append(piece.reshape(shape))
        offset += rows
    return outs


def absorb(carry, queries, keys, values, valid):
    top, total, accum = carry
    scores = jnp.einsum("qhd,khd->hqk", queries, keys, preferred_element_type=jnp.float32) * HD ** (
        -0.5
    )
    scores = jnp.where(valid[None], scores, NEG_FILL)
    new_top = jnp.maximum(top, jnp.max(scores, axis=-1, keepdims=True))
    factor = jnp.exp(top - new_top)
    probs = jnp.where(valid[None], jnp.exp(scores - new_top), 0.0)
    total = total * factor + jnp.sum(probs, axis=-1, keepdims=True)
    accum = accum * factor + jnp.einsum(
        "hqk,khd->hqd", probs.astype(jnp.bfloat16), values, preferred_element_type=jnp.float32
    )
    return (new_top, total, accum)


def on_device(
    hidden_in, w_qkv, w_out, attn_gain, mlp_gain, w_gate, w_up, w_down, k_cache, v_cache, cache_len
):
    new_count = hidden_in.shape[0]
    w_qkv_full = lax.all_gather(w_qkv, "req", axis=1, tiled=True)
    w_gate_full, w_up_full, w_down_full, w_out_full = gather_packed(
        [w_gate, w_up, w_down, w_out], [0, 0, 1, 1], "req"
    )
    width = w_qkv.shape[2]
    heads_local = width // HD
    slots = k_cache.shape[1]
    full_rows = lax.all_gather(hidden_in, "mp", axis=1, tiled=True)
    normed = rms_scale(full_rows, attn_gain)
    columns = normed
    projected = jnp.einsum("nd,kdw->knw", columns, w_qkv_full, preferred_element_type=jnp.float32)
    length = cache_len[0]
    positions = (length + jnp.arange(new_count, dtype=jnp.int32)).astype(jnp.float32)
    queries = rotate(projected[0].reshape(new_count, heads_local, HD), positions).astype(
        jnp.bfloat16
    )
    fresh_keys = rotate(projected[1].reshape(new_count, heads_local, HD), positions).astype(
        jnp.bfloat16
    )
    fresh_values = projected[2].astype(jnp.bfloat16).reshape(new_count, heads_local, HD)
    rows = jnp.arange(new_count, dtype=jnp.int32)
    causal = rows[:, None] >= rows[None, :]
    start_carry = (
        jnp.full((heads_local, new_count, 1), NEG_FILL, jnp.float32),
        jnp.zeros((heads_local, new_count, 1), jnp.float32),
        jnp.zeros((heads_local, new_count, HD), jnp.float32),
    )
    carry = absorb(start_carry, queries, fresh_keys, fresh_values, causal)
    cache_keys = k_cache[0].reshape(slots, heads_local, HD)
    cache_values = v_cache[0].reshape(slots, heads_local, HD)
    block = min(slots, 512)
    count = (length + block - 1) // block

    def step_block(index, state):
        begin = index * block
        keys = lax.dynamic_slice_in_dim(cache_keys, begin, block, 0)
        values = lax.dynamic_slice_in_dim(cache_values, begin, block, 0)
        valid = (begin + jnp.arange(block, dtype=jnp.int32) < length)[None, :]
        return absorb(state, queries, keys, values, valid)

    top, total, accum = lax.fori_loop(0, count, step_block, carry)
    attn = (accum / total).transpose(1, 0, 2).reshape(new_count, width).astype(jnp.bfloat16)
    partial_value = jnp.dot(attn, w_out_full, preferred_element_type=jnp.float32)
    summed = lax.psum(partial_value.astype(jnp.bfloat16), "mp").astype(jnp.float32)
    mid_full = (full_rows.astype(jnp.float32) + summed).astype(jnp.bfloat16)
    own = hidden_in.shape[1]
    mid_local = lax.dynamic_slice_in_dim(mid_full, lax.axis_index("mp") * own, own, axis=1)
    normed2 = rms_scale(mid_full, mlp_gain)
    columns = normed2
    gate = jnp.dot(columns, w_gate_full, preferred_element_type=jnp.float32)
    upper = jnp.dot(columns, w_up_full, preferred_element_type=jnp.float32)
    units = (jax.nn.silu(gate) * upper).astype(jnp.bfloat16)
    terms = jnp.dot(units, w_down_full, preferred_element_type=jnp.float32)
    reduced = lax.psum_scatter(
        terms.astype(jnp.bfloat16), "mp", scatter_dimension=1, tiled=True
    ).astype(jnp.float32)
    hidden_out = (mid_local.astype(jnp.float32) + reduced).astype(jnp.bfloat16)
    return (
        hidden_out,
        fresh_keys.reshape(new_count, width),
        fresh_values.reshape(new_count, width),
    )


def solution(mesh):
    return jax.shard_map(
        on_device,
        mesh=mesh,
        in_specs=(
            P("req", "mp"),
            P(None, "req", "mp"),
            P("mp", "req"),
            P(),
            P(),
            P("req", "mp"),
            P("req", "mp"),
            P("mp", "req"),
            P("req", None, "mp"),
            P("req", None, "mp"),
            P("req"),
        ),
        out_specs=(P("req", "mp"), P("req", "mp"), P("req", "mp")),
        check_vma=False,
    )
```

profile of v0, /device:TPU:0, one launch (start us, length us, event | category | flops | bytes accessed | tf_op | source)
XLA Modules:
  0.0 353.1 jit_solution(15132475671423839923)
XLA Ops:
  7.2 0.7 all-gather.5.cloned.1.call-update
  8.0 1.7 copy.29
  9.7 0.0 all-gather.9.cloned.1.call-start
  9.8 1.1 reshape.167
  10.8 1.1 reshape.168
  11.9 2.0 pad_maximum_fusion
  14.6 2.9 copy.31
  17.6 4.1 %copy.32 = bf16[1,4096,256]{1,2,0:T(8,128)(2,1)} copy(bf16[1,4096,256]{2,1,0:T(8,128)(2,1)} %param.22) | data formatting | bytes 4194304 | tf_op args[9]
  21.7 1.3 iota_compare_fusion
  23.0 0.5 multiply_cosine_fusion
  23.5 24.7 %all-gather.5.cloned.1.call-done = bf16[1024,2048]{1,0:T(8,128)(2,1)} async-done(((bf16[1024,256]{1,0:T(8,128)(2,1)}), bf16[1024,2048]{1,0:T(8,128)(2,1)}) %all-gather.5.cloned.1.call-update) | async-done | bytes 4194320 | tf_op jit(solution)/shard_map/all_gather | solution.py:76
  48.2 3.1 fusion.26
  51.3 53.4 %all-gather.7.cloned.1.call-done = bf16[3,2048,256]{1,2,0:T(8,128)(2,1)} async-done(((bf16[3,128,256]{1,2,0:T(8,128)(2,1)}), bf16[3,2048,256]{1,2,0:T(8,128)(2,1)}) %all-gather.7.cloned.1.call-update) | async-done | bytes 3145744 | tf_op jit(solution)/shard_map/all_gather | solution.py:69
  104.7 6.6 %fusion.38 = f32[3,1024,256]{1,2,0:T(8,128)S(1)} fusion(bf16[3,2048,256]{1,2,0:T(8,128)(2,1)} %all-gather.7.cloned.1.call-done, bf16[1024,2048]{1,0:T(8,128)(2,1)} %all-gather.5.cloned.1.call-done, f32[2048]{0:T(1024)S(1)} %convert_element_type.84, f32[1024]{0:T(1024)S(1)} %add_rsqrt_fusion.1), kind=kOutput, calls=%fused_computation.52 | convolution fusion | flops 3229614080 | bytes 10498048 | tf_op jit(solution)/shard_map/nd,kdw->knw/dot_general | solution.py:79
  111.3 1.0 slice.66
  112.3 0.1 fusion.57
  112.4 0.2 subtract_convert_fusion
  112.6 0.2 multiply_subtract_fusion
  112.8 0.3 copy-done.3
  113.1 0.7 copy-done.1
  113.8 3.0 fusion.20
  116.8 4.2 %fusion.22 = f32[4,1024]{1,0:T(4,128)S(1)} fusion(f32[4,1024,1024]{1,2,0:T(8,128)S(1)} %get-tuple-element.102, f32[4,1024]{1,0:T(4,128)S(1)} %get-tuple-element.98, pred[1024,1024]{0,1:T(8,128)(4,1)S(1)} %copy-done.1), kind=kLoop, calls=%fused_computation.31 | loop fusion | flops 20967424 | bytes 17858560 | tf_op jit(solution)/shard_map/reduce_sum | solution.py:58
  121.1 5.9 %fusion.41 = f32[4,1024,64]{1,2,0:T(8,128)} fusion(bf16[1024,4,64]{0,2,1:T(8,128)(2,1)S(1)} %bitcast.91, f32[4,1024,1024]{1,2,0:T(8,128)S(1)} %get-tuple-element.102, f32[4,1024]{1,0:T(4,128)S(1)} %get-tuple-element.98, pred[1024,1024]{0,1:T(8,128)(4,1)S(1)} %copy-done.1, f32[4,1024]{1,0:T(4,128)S(1)} %get-tuple-element.96), kind=kOutput, calls=%fused_computation.53 | convolution fusion | flops 558104576 | bytes 19431424 | tf_op jit(solution)/shard_map/hqk,khd->hqd/dot_general | solution.py:59
  127.0 8.0 %while.14 = (s32[]{:T(128)}, f32[4,1024,1]{1,0,2:T(4,128)S(1)}, f32[4,1024,1]{1,0,2:T(4,128)S(1)}, f32[4,1024,64]{1,2,0:T(8,128)}, s32[]{:T(128)}, /*index=5*/s3...) while((s32[]{:T(128)}, f32[4,1024,1]{1,0,2:T(4,128)S(1)}, ...), condition=%wide.region_6.7_spmd, body=%wide.region_3.6_spmd.sunk | while | flops 564671488 | bytes 36965104 | solution.py:109
  127.0 0.7 add_compare_fusion.2
  127.7 1.6 bitcast_reduce_fusion.2
  129.3 3.1 fusion.77
  132.4 2.5 fusion.76
  135.0 1.3 divide_convert_fusion
  136.3 65.2 %all-gather.9.cloned.1.call-done = bf16[53248,128]{1,0:T(8,128)(2,1)} async-done(((bf16[3328,128]{1,0:T(8,128)(2,1)}), bf16[53248,128]{1,0:T(8,128)(2,1)}) %all-gather.9.cloned.1.call-update) | async-done | bytes 13631504 | tf_op jit(solution)/shard_map/all_gather | solution.py:35
  201.5 1.3 slice_bitcast_fusion.1
  202.8 0.5 copy.33
  203.4 3.3 convolution_convert_fusion
  206.7 0.3 reduce-scatter.2.cloned.1.call-start
  207.0 0.4 copy-done.8
  207.4 9.1 %fusion.56 = (bf16[16,1024,128]{2,1,0:T(8,128)(2,1)}, bf16[1024,16,128]{2,0,1:T(8,128)(2,1)}, bf16[16,1024,128]{2,1,0:T(8,128)(2,1)}) fusion(bf16[16,3328,128]{2,1,0:T(8,128)(2,1)} %bitcast.79), kind=kLoop, calls=%fused_computation.81 | loop fusion | bytes 25165824 | tf_op jit(solution)/shard_map/slice | solution.py:40
  216.5 7.4 %reshape_reshape.6 = bf16[2048,1024]{1,0:T(8,128)(2,1)} reshape(bf16[16,1024,128]{2,1,0:T(8,128)(2,1)} %get-tuple-element.89) | data formatting | bytes 8388608 | tf_op jit(solution)/shard_map/reshape;reshape | solution.py:44
  223.9 6.4 %copy.34 = bf16[1024,16,128]{0,2,1:T(8,128)(2,1)} copy(bf16[1024,16,128]{2,0,1:T(8,128)(2,1)} %get-tuple-element.88) | data formatting | bytes 8388608 | tf_op jit(solution)/shard_map/transpose | solution.py:41
  230.4 7.4 %reshape_reshape.7 = bf16[2048,1024]{1,0:T(8,128)(2,1)} reshape(bf16[16,1024,128]{2,1,0:T(8,128)(2,1)} %get-tuple-element.87) | data formatting | bytes 8388608 | tf_op jit(solution)/shard_map/reshape;reshape | solution.py:44
  237.8 41.3 %all-reduce.2.cloned.1.call-done = bf16[1024,2048]{1,0:T(8,128)(2,1)} async-done(((bf16[1024,2048]{1,0:T(8,128)(2,1)}), bf16[1024,2048]{1,0:T(8,128)(2,1)}) %all-reduce.2.cloned.1.call-update) | async-done | bytes 4194320 | tf_op jit(solution)/shard_map/psum | solution.py:112
  279.0 5.6 %fusion.23 = (f32[1024]{0:T(1024)S(1)}, bf16[1024,2048]{1,0:T(8,128)(2,1)S(1)}) fusion(bf16[1024,2048]{1,0:T(8,128)(2,1)} %all-reduce.2.cloned.1.call-done, bf16[1024,2048]{1,0:T(8,128)(2,1)} %all-gather.5.cloned.1.call-done), kind=kLoop, calls=%fused_computation.34 | loop fusion | flops 14679040 | bytes 12587008 | tf_op jit(solution)/shard_map/reduce_sum | solution.py:14
  284.7 6.3 %fusion.45 = f32[1024,1024]{1,0:T(8,128)} fusion(bf16[2048,1024]{1,0:T(8,128)(2,1)S(1)} %copy-done.2, bf16[1024,2048]{1,0:T(8,128)(2,1)S(1)} %get-tuple-element.84, f32[2048]{0:T(1024)S(1)} %convert_element_type.99, f32[1024]{0:T(1024)S(1)} %add_rsqrt_fusion), kind=kOutput, calls=%fused_computation.54 | convolution fusion | flops 4303355904 | bytes 12595200 | tf_op jit(solution)/shard_map/dot_general | solution.py:118
  291.0 15.4 %convolution_convert_fusion.1 = bf16[1024,2048]{1,0:T(8,128)(2,1)} fusion(bf16[1024,2048]{0,1:T(8,128)(2,1)} %bitcast.84, f32[1024,1024]{1,0:T(8,128)} %fusion.45, bf16[2048,1024]{1,0:T(8,128)(2,1)} %reshape_reshape.7, bf16[1024,2048]{1,0:T(8,128)(2,1)} %copy-done, f32[2048]{0:T(1024)S(1)} %convert_element_type.99, f32[1024]{0:T(1024)S(1)} %add_rsqrt_fusion), kind=kOutput, calls=%fused_computation.51 | convolution fusion | flops 8606711808 | bytes 20983808 | tf_op jit(solution)/shard_map/dot_general | solution.py:121
  306.4 1.0 copy.35
  307.4 1.3 slice_bitcast_fusion.2
  308.7 1.0 copy.36
  309.7 34.8 %reduce-scatter.2.cloned.1.call-done = bf16[1024,256]{1,0:T(8,128)(2,1)} async-done(((bf16[1024,2048]{1,0:T(8,128)(2,1)}), bf16[1024,256]{1,0:T(8,128)(2,1)}) %reduce-scatter.2.cloned.1.call-update) | async-done | bytes 524304 | tf_op jit(solution)/shard_map/reduce_scatter | solution.py:122
  344.5 2.1 add_convert_fusion
  (35 shorter events, 0.4 us)
Async XLA Ops:
  7.2 7.4 %copy-start.7 = (bf16[2048]{0:T(1024)(128)(2,1)S(1)}, bf16[2048]{0:T(1024)(128)(2,1)}, u32[]{:S(2)}) copy-start(bf16[2048]{0:T(1024)(128)(2,1)} %param.16) | copy-start | bytes 12292
  7.2 41.0 %all-gather.5.cloned.1.call-start = ((), (), s32[]{:S(2)}) async-start(), calls=%async_computation.1 | async-start | bytes 4718592 | tf_op jit(solution)/shard_map/all_gather | solution.py:76
  7.9 96.8 %all-gather.7.cloned.1.call-start = ((), (), s32[]{:S(2)}) async-start(), calls=%async_computation.2 | async-start | bytes 3342336 | tf_op jit(solution)/shard_map/all_gather | solution.py:69
  9.7 191.8 %all-gather.9.cloned.1.call-start = ((), (), s32[]{:S(2)}) async-start(), calls=%async_computation.5 | async-start | bytes 14483456 | tf_op jit(solution)/shard_map/all_gather | solution.py:35
  13.9 265.1 %all-reduce.2.cloned.1.call-start = ((), (), s32[]{:S(2)}) async-start(), calls=%async_computation.3 | async-start | bytes 8388608 | tf_op jit(solution)/shard_map/psum | solution.py:112
  111.3 1.8 copy-start.3
  112.3 1.5 copy-start.1
  116.8 4.2 %copy-start.6 = (bf16[1,1024,256]{1,2,0:T(8,128)(2,1)S(1)}, bf16[1,1024,256]{1,2,0:T(8,128)(2,1)}, u32[]{:S(2)}) copy-start(bf16[1,1024,256]{1,2,0:T(8,128)(2,1)} %slice.66) | copy-start | bytes 1572868
  127.7 1.6 copy-start.4
  132.4 2.6 copy-start.5
  206.7 0.7 copy-start.8
  206.7 137.7 %reduce-scatter.2.cloned.1.call-start = ((), (), s32[]{:S(2)}) async-start(), calls=%async_computation.4 | async-start | bytes 4718592 | tf_op jit(solution)/shard_map/reduce_scatter | solution.py:122
  279.0 5.6 %copy-start.2 = (bf16[2048,1024]{1,0:T(8,128)(2,1)S(1)}, bf16[2048,1024]{1,0:T(8,128)(2,1)}, u32[]{:S(2)}) copy-start(bf16[2048,1024]{1,0:T(8,128)(2,1)} %reshape_reshape.6) | copy-start | bytes 12582916
  284.6 6.4 %copy-start = (bf16[1024,2048]{1,0:T(8,128)(2,1)}, bf16[1024,2048]{1,0:T(8,128)(2,1)S(1)}, u32[]{:S(2)}) copy-start(bf16[1024,2048]{1,0:T(8,128)(2,1)S(1)} %get-tuple-element.84) | copy-start | bytes 12582916
Sparse Core Ops, SparseCore 0:
  9.7 38.4 all-gather.4
  50.9 53.7 all-gather.6
  106.9 94.6 all-gather.8
  206.9 72.1 all-reduce.1
  306.5 37.9 reduce-scatter.1
where the time goes:
time: 354 us; the launch traced here: 353 us
  waiting for transfers between devices  220 us (62%)
  local copies, waits for them, and re-layouts  48.9 us (14%)
  matrix products  45.3 us (13%)
  other arithmetic  23.8 us (7%)
  between operations  14.7 us (4%)
    all_gather x1, waiting for transfers between devices, gather_packed(): gathered = lax.all_gather(joined, axis_name, axis=0, tiled=False)  65.2 us
    all_gather x1, waiting for transfers between devices, on_device(): w_qkv_full = lax.all_gather(w_qkv, 'req', axis=1, tiled=True)  53.4 us
    psum x1, waiting for transfers between devices, on_device(): lax.psum(partial_value.astype(jnp.bfloat16), 'mp').astype(jnp.float32)  41.3 us
    reduce_scatter x1, waiting for transfers between devices, on_device(): lax.psum_scatter(terms.astype(jnp.bfloat16), 'mp', scatter_dimension=1, t...  34.8 us
    all_gather x1, waiting for transfers between devices, on_device(): full_rows = lax.all_gather(hidden_in, 'mp', axis=1, tiled=True)  24.7 us
    dot_general x1, matrix products, on_device(): terms = jnp.dot(units, w_down_full, preferred_element_type=jnp.float32)  15.4 us
    another operation x2, local copies, waits for them, and re-layouts, gather_packed(): outs.append(piece.reshape(shape))  14.8 us
    unnamed x19, local copies, waits for them, and re-layouts  12.2 us
  transfers between devices with their start and end apart: 5, of which 5 were waited for; matrix products, arithmetic and copies ran while one was open for 23% of the time, Pallas kernels for 0%

commit v1 on v0

--- a/solution.py
+++ b/solution.py
@@ -73,7 +73,9 @@
     width = w_qkv.shape[2]
     heads_local = width // HD
     slots = k_cache.shape[1]
-    full_rows = lax.all_gather(hidden_in, "mp", axis=1, tiled=True)
+    full_rows = jnp.concatenate(
+        lax.all_to_all(jnp.stack([hidden_in] * lax.axis_size("mp")), "mp", 0, 0), axis=1
+    )
     normed = rms_scale(full_rows, attn_gain)
     columns = normed
     projected = jnp.einsum("nd,kdw->knw", columns, w_qkv_full, preferred_element_type=jnp.float32)

time: 354 us -> 322 us (0.910)
  waiting for transfers between devices: 220 us -> 172 us
  local copies, waits for them, and re-layouts: 48.9 us -> 55.6 us
  starting transfers between devices: 0.42 us -> 4.88 us
  other arithmetic: 23.8 us -> 27.5 us
    all_gather x1, waiting for transfers between devices: 53.4 us -> 0.02 us  [on_device(): w_qkv_full = lax.all_gather(w_qkv, 'req', axis=1, tiled=True)]
    all_to_all x0 -> x1, waiting for transfers between devices: none -> 40 us  [on_device(): lax.all_to_all(jnp.stack([hidden_in] * lax.axis_size('mp')), 'mp', 0, 0)]
    all_gather x1 -> x0, waiting for transfers between devices: 24.7 us -> none  [on_device(): full_rows = lax.all_gather(hidden_in, 'mp', axis=1, tiled=True)]
    all_gather x1, waiting for transfers between devices: 65.2 us -> 49.7 us  [gather_packed(): gathered = lax.all_gather(joined, axis_name, axis=0, tiled=False)]
    psum x1, waiting for transfers between devices: 41.3 us -> 47.2 us  [on_device(): lax.psum(partial_value.astype(jnp.bfloat16), 'mp').astype(jnp.float32)]
    all_to_all x0 -> x1, starting transfers between devices: none -> 4.71 us  [on_device(): lax.all_to_all(jnp.stack([hidden_in] * lax.axis_size('mp')), 'mp', 0, 0)]
    convert_element_type x0 -> x1, local copies, waits for them, and re-layouts: none -> 4.28 us  [on_device(): mid_full = (full_rows.astype(jnp.float32) + summed).astype(jnp.bfloat16)]
    unnamed x19 -> x21, local copies, waits for them, and re-layouts: 12.2 us -> 12.4 us
  transfers between devices with their start and end apart: 5 -> 5, of which waited for: 5 -> 4; matrix products, arithmetic and copies ran while one was open for 23% -> 28% of each run, Pallas kernels for 0% -> 0%
where the time goes in v1:
time: 322 us; the launch traced here: 321 us
  waiting for transfers between devices  172 us (53%)
  local copies, waits for them, and re-layouts  55.6 us (17%)
  matrix products  46.1 us (14%)
  other arithmetic  27.5 us (9%)
  between operations  14.7 us (5%)
  starting transfers between devices  4.88 us (2%)
    all_gather x1, waiting for transfers between devices, gather_packed(): gathered = lax.all_gather(joined, axis_name, axis=0, tiled=False)  49.7 us
    psum x1, waiting for transfers between devices, on_device(): lax.psum(partial_value.astype(jnp.bfloat16), 'mp').astype(jnp.float32)  47.2 us
    all_to_all x1, waiting for transfers between devices, on_device(): lax.all_to_all(jnp.stack([hidden_in] * lax.axis_size('mp')), 'mp', 0, 0)  40 us
    reduce_scatter x1, waiting for transfers between devices, on_device(): lax.psum_scatter(terms.astype(jnp.bfloat16), 'mp', scatter_dimension=1, t...  34.8 us
    dot_general x1, matrix products, on_device(): terms = jnp.dot(units, w_down_full, preferred_element_type=jnp.float32)  15.4 us
    another operation x2, local copies, waits for them, and re-layouts, gather_packed(): outs.append(piece.reshape(shape))  14.8 us
    unnamed x21, local copies, waits for them, and re-layouts  12.4 us
    reduce_sum x2, other arithmetic, rms_scale(): meansq = jnp.mean(values * values, axis=-1, keepdims=True)  9.45 us
  transfers between devices with their start and end apart: 5, of which 4 were waited for; matrix products, arithmetic and copies ran while one was open for 28% of the time, Pallas kernels for 0%

profile of v1, /device:TPU:0, one launch (start us, length us, event | category | flops | bytes accessed | tf_op | source)
XLA Modules:
  0.0 320.7 jit_solution(11449471889414298141)
XLA Ops:
  7.2 1.8 copy.39
  9.1 1.1 reshape.173
  10.2 1.1 reshape.174
  11.2 2.0 pad_maximum_fusion
  13.2 2.2 stack.2
  15.4 4.7 %all-to-all-start = ((bf16[8,1024,256]{2,1,0:T(8,128)(2,1)}), bf16[8,1024,256]{2,1,0:T(8,128)(2,1)}, u32[]{:S(2)}, u32[]{:S(2)}) async-start(bf16[8,1024,256]{2,1,0:T(8,128)(2,1)} %stack.2), calls=%async_computation | async-start | bytes 8388608 | tf_op jit(solution)/shard_map/all_to_all | solution.py:77
  20.9 2.9 copy.41
  23.9 4.1 %copy.42 = bf16[1,4096,256]{1,2,0:T(8,128)(2,1)} copy(bf16[1,4096,256]{2,1,0:T(8,128)(2,1)} %param.22) | data formatting | bytes 4194304 | tf_op args[9]
  28.0 1.3 iota_compare_fusion
  29.3 0.5 multiply_cosine_fusion
  29.8 40.0 %all-to-all-done = bf16[8,1024,256]{2,1,0:T(8,128)(2,1)} async-done(((bf16[8,1024,256]{2,1,0:T(8,128)(2,1)}), bf16[8,1024,256]{2,1,0:T(8,128)(2,1)}, u32[]{:S(2)}, u32[]{:S(2)}) %all-to-all-start) | async-done | bytes 4194336 | tf_op jit(solution)/shard_map/all_to_all | solution.py:77
  69.8 2.9 convert_bitcast_fusion
  72.8 4.3 %copy.49 = f32[8,128,8,256]{3,2,0,1:T(8,128)} copy(f32[8,128,8,256]{3,2,1,0:T(8,128)S(1)} %convert_bitcast_fusion) | data formatting | bytes 16777216 | tf_op jit(solution)/shard_map/convert_element_type | solution.py:115
  77.1 3.4 %fusion.26 = f32[1024]{0:T(1024)S(1)} fusion(bf16[8,1024,256]{2,1,0:T(8,128)(2,1)} %all-to-all-done), kind=kLoop, calls=%fused_computation.36 | loop fusion | flops 6290432 | bytes 4198400 | tf_op jit(solution)/shard_map/reduce_sum | solution.py:14
  80.5 7.3 %fusion.35 = f32[3,1024,256]{1,2,0:T(8,128)S(1)} fusion(bf16[3,2048,256]{1,2,0:T(8,128)(2,1)} %all-gather.4.cloned.1.call-done, f32[1024,2048]{1,0:T(8,128)} %bitcast.82, f32[2048]{0:T(1024)S(1)} %convert_element_type.97, f32[1024]{0:T(1024)S(1)} %add_rsqrt_fusion.1), kind=kOutput, calls=%fused_computation.50 | convolution fusion | flops 3227516928 | bytes 14692352 | tf_op jit(solution)/shard_map/nd,kdw->knw/dot_general | solution.py:81
  87.8 1.0 slice.66
  88.9 0.2 fusion.53
  89.1 0.2 subtract_convert_fusion
  89.3 0.2 multiply_subtract_fusion
  89.5 0.2 copy-done.3
  89.6 0.7 copy-done.1
  90.3 3.0 fusion.20
  93.4 4.2 %fusion.22 = f32[4,1024]{1,0:T(4,128)S(1)} fusion(f32[4,1024,1024]{1,2,0:T(8,128)S(1)} %get-tuple-element.105, f32[4,1024]{1,0:T(4,128)S(1)} %get-tuple-element.101, pred[1024,1024]{0,1:T(8,128)(4,1)S(1)} %copy-done.1), kind=kLoop, calls=%fused_computation.28 | loop fusion | flops 20967424 | bytes 17858560 | tf_op jit(solution)/shard_map/reduce_sum | solution.py:58
  97.6 6.2 %fusion.38 = f32[4,1024,64]{1,2,0:T(8,128)} fusion(bf16[1024,4,64]{0,2,1:T(8,128)(2,1)S(1)} %bitcast.97, f32[4,1024,1024]{1,2,0:T(8,128)S(1)} %get-tuple-element.105, f32[4,1024]{1,0:T(4,128)S(1)} %get-tuple-element.101, pred[1024,1024]{0,1:T(8,128)(4,1)S(1)} %copy-done.1, f32[4,1024]{1,0:T(4,128)S(1)} %get-tuple-element.99), kind=kOutput, calls=%fused_computation.51 | convolution fusion | flops 558104576 | bytes 19431424 | tf_op jit(solution)/shard_map/hqk,khd->hqd/dot_general | solution.py:59
  103.8 8.0 %while.14 = (s32[]{:T(128)}, f32[4,1024,1]{1,0,2:T(4,128)S(1)}, f32[4,1024,1]{1,0,2:T(4,128)S(1)}, f32[4,1024,64]{1,2,0:T(8,128)}, s32[]{:T(128)}, /*index=5*/s3...) while((s32[]{:T(128)}, f32[4,1024,1]{1,0,2:T(4,128)S(1)}, ...), condition=%wide.region_6.7_spmd, body=%wide.region_3.6_spmd.sunk | while | flops 564671488 | bytes 36965104 | solution.py:111
  103.8 0.7 add_compare_fusion.2
  104.5 1.6 bitcast_reduce_fusion.2
  106.1 3.1 fusion.73
  109.2 2.5 fusion.72
  111.8 1.3 divide_convert_fusion
  113.1 49.7 %all-gather.6.cloned.1.call-done = bf16[53248,128]{1,0:T(8,128)(2,1)} async-done(((bf16[3328,128]{1,0:T(8,128)(2,1)}), bf16[53248,128]{1,0:T(8,128)(2,1)}) %all-gather.6.cloned.1.call-update) | async-done | bytes 13631504 | tf_op jit(solution)/shard_map/all_gather | solution.py:35
  162.8 1.3 slice_bitcast_fusion.1
  164.1 0.5 copy.43
  164.6 3.4 %convolution_convert_fusion = bf16[1024,2048]{1,0:T(8,128)(2,1)} fusion(bf16[1024,256]{0,1:T(8,128)(2,1)S(1)} %bitcast.93, bf16[256,2048]{0,1:T(8,128)(2,1)S(1)} %bitcast.89), kind=kOutput, calls=%fused_computation.48 | convolution fusion | flops 1075838976 | bytes 5767168 | tf_op jit(solution)/shard_map/dot_general | solution.py:113
  168.1 0.6 copy-done.9
  168.7 9.0 %fusion.52 = (bf16[16,1024,128]{2,1,0:T(8,128)(2,1)}, bf16[1024,16,128]{2,0,1:T(8,128)(2,1)}, bf16[16,1024,128]{2,1,0:T(8,128)(2,1)}) fusion(bf16[16,3328,128]{2,1,0:T(8,128)(2,1)} %bitcast.85), kind=kLoop, calls=%fused_computation.79 | loop fusion | bytes 25165824 | tf_op jit(solution)/shard_map/slice | solution.py:40
  177.7 7.4 %reshape_reshape.6 = bf16[2048,1024]{1,0:T(8,128)(2,1)} reshape(bf16[16,1024,128]{2,1,0:T(8,128)(2,1)} %get-tuple-element.92) | data formatting | bytes 8388608 | tf_op jit(solution)/shard_map/reshape;reshape | solution.py:44
  185.2 6.4 %copy.44 = bf16[1024,16,128]{0,2,1:T(8,128)(2,1)} copy(bf16[1024,16,128]{2,0,1:T(8,128)(2,1)} %get-tuple-element.91) | data formatting | bytes 8388608 | tf_op jit(solution)/shard_map/transpose | solution.py:41
  191.6 7.4 %reshape_reshape.7 = bf16[2048,1024]{1,0:T(8,128)(2,1)} reshape(bf16[16,1024,128]{2,1,0:T(8,128)(2,1)} %get-tuple-element.90) | data formatting | bytes 8388608 | tf_op jit(solution)/shard_map/reshape;reshape | solution.py:44
  199.0 47.2 %all-reduce.2.cloned.1.call-done = bf16[1024,2048]{1,0:T(8,128)(2,1)} async-done(((bf16[1024,2048]{1,0:T(8,128)(2,1)}), bf16[1024,2048]{1,0:T(8,128)(2,1)}) %all-reduce.2.cloned.1.call-update) | async-done | bytes 4194320 | tf_op jit(solution)/shard_map/psum | solution.py:114
  246.2 6.0 %fusion.23 = (f32[1024]{0:T(1024)S(1)}, bf16[1024,2048]{1,0:T(8,128)(2,1)S(1)}) fusion(f32[1024,2048]{1,0:T(8,128)} %bitcast.83, bf16[1024,2048]{1,0:T(8,128)(2,1)} %all-reduce.2.cloned.1.call-done), kind=kLoop, calls=%fused_computation.33 | loop fusion | flops 12581888 | bytes 16781312 | tf_op jit(solution)/shard_map/reduce_sum | solution.py:14
  252.3 6.3 %fusion.42 = f32[1024,1024]{1,0:T(8,128)} fusion(bf16[2048,1024]{1,0:T(8,128)(2,1)S(1)} %copy-done.2, bf16[1024,2048]{1,0:T(8,128)(2,1)S(1)} %get-tuple-element.87, f32[2048]{0:T(1024)S(1)} %convert_element_type.112, f32[1024]{0:T(1024)S(1)} %add_rsqrt_fusion), kind=kOutput, calls=%fused_computation.52 | convolution fusion | flops 4303355904 | bytes 12595200 | tf_op jit(solution)/shard_map/dot_general | solution.py:120
  258.5 15.4 %convolution_convert_fusion.1 = bf16[1024,2048]{1,0:T(8,128)(2,1)} fusion(bf16[1024,2048]{0,1:T(8,128)(2,1)} %bitcast.90, f32[1024,1024]{1,0:T(8,128)} %fusion.42, bf16[2048,1024]{1,0:T(8,128)(2,1)} %reshape_reshape.7, bf16[1024,2048]{1,0:T(8,128)(2,1)} %copy-done, f32[2048]{0:T(1024)S(1)} %convert_element_type.112, f32[1024]{0:T(1024)S(1)} %add_rsqrt_fusion), kind=kOutput, calls=%fused_computation.49 | convolution fusion | flops 8606711808 | bytes 20983808 | tf_op jit(solution)/shard_map/dot_general | solution.py:123
  274.0 1.0 copy.45
  275.0 1.3 slice_bitcast_fusion.2
  276.3 1.0 copy.46
  277.3 34.8 %reduce-scatter.2.cloned.1.call-done = bf16[1024,256]{1,0:T(8,128)(2,1)} async-done(((bf16[1024,2048]{1,0:T(8,128)(2,1)}), bf16[1024,256]{1,0:T(8,128)(2,1)}) %reduce-scatter.2.cloned.1.call-update) | async-done | bytes 524304 | tf_op jit(solution)/shard_map/reduce_scatter | solution.py:124
  312.1 2.1 add_convert_fusion.1
  (39 shorter events, 0.5 us)
Async XLA Ops:
  7.2 6.1 %copy-start.6 = (bf16[1024,256]{1,0:T(8,128)(2,1)S(1)}, bf16[1024,256]{1,0:T(8,128)(2,1)}, u32[]{:S(2)}) copy-start(bf16[1024,256]{1,0:T(8,128)(2,1)} %param.13) | copy-start | bytes 1572868
  7.2 73.4 %all-gather.4.cloned.1.call-start = ((), (), s32[]{:S(2)}) async-start(), calls=%async_computation.2 | async-start | bytes 3342336 | tf_op jit(solution)/shard_map/all_gather | solution.py:69
  9.0 153.7 %all-gather.6.cloned.1.call-start = ((), (), s32[]{:S(2)}) async-start(), calls=%async_computation.5 | async-start | bytes 14483456 | tf_op jit(solution)/shard_map/all_gather | solution.py:35
  15.4 5.4 %copy-start.8 = (bf16[2048]{0:T(1024)(128)(2,1)S(1)}, bf16[2048]{0:T(1024)(128)(2,1)}, u32[]{:S(2)}) copy-start(bf16[2048]{0:T(1024)(128)(2,1)} %param.16) | copy-start | bytes 12292
  15.4 54.4 %all-to-all-start = ((bf16[8,1024,256]{2,1,0:T(8,128)(2,1)}), bf16[8,1024,256]{2,1,0:T(8,128)(2,1)}, u32[]{:S(2)}, u32[]{:S(2)}) async-start(bf16[8,1024,256]{2,1,0:T(8,128)(2,1)} %stack.2), calls=%async_computation | async-start | bytes 8388608 | tf_op jit(solution)/shard_map/all_to_all | solution.py:77
  20.2 226.0 %all-reduce.2.cloned.1.call-start = ((), (), s32[]{:S(2)}) async-start(), calls=%async_computation.3 | async-start | bytes 8388608 | tf_op jit(solution)/shard_map/psum | solution.py:114
  87.8 1.8 copy-start.3
  88.9 1.5 copy-start.1
  93.4 4.2 %copy-start.7 = (bf16[1,1024,256]{1,2,0:T(8,128)(2,1)S(1)}, bf16[1,1024,256]{1,2,0:T(8,128)(2,1)}, u32[]{:S(2)}) copy-start(bf16[1,1024,256]{1,2,0:T(8,128)(2,1)} %slice.66) | copy-start | bytes 1572868
  104.5 1.6 copy-start.4
  109.2 2.6 copy-start.5
  168.0 0.7 copy-start.9
  168.1 144.0 %reduce-scatter.2.cloned.1.call-start = ((), (), s32[]{:S(2)}) async-start(), calls=%async_computation.4 | async-start | bytes 4718592 | tf_op jit(solution)/shard_map/reduce_scatter | solution.py:124
  246.2 6.0 %copy-start.2 = (bf16[2048,1024]{1,0:T(8,128)(2,1)S(1)}, bf16[2048,1024]{1,0:T(8,128)(2,1)}, u32[]{:S(2)}) copy-start(bf16[2048,1024]{1,0:T(8,128)(2,1)} %reshape_reshape.6) | copy-start | bytes 12582916
  252.2 6.3 %copy-start = (bf16[1024,2048]{1,0:T(8,128)(2,1)}, bf16[1024,2048]{1,0:T(8,128)(2,1)S(1)}, u32[]{:S(2)}) copy-start(bf16[1024,2048]{1,0:T(8,128)(2,1)S(1)} %get-tuple-element.87) | copy-start | bytes 12582916
Sparse Core Ops, SparseCore 0:
  10.7 55.1 all-gather.3
  68.1 94.6 all-gather.5
  168.2 77.9 all-reduce.1
  274.0 37.9 reduce-scatter.1
